TPU v7x, 256 devices: a whole 4x4x8 slice. The times are simulated.
256 devices in a mesh: scan: 8 (over x, core), mode: 32 (over y, z).
Axes of the slice: x: 4, y: 4, z: 8, core: 2. Of those that a mesh axis runs over, the one named last changes fastest.
Arguments:
- object_field: float32 [2, 2048, 1024], P(None, 'scan'), may hold values from -5 to 5
- probe_modes: float32 [2, 32, 128, 128], P(None, 'mode'), may hold values from -9 to 9
- scan_offsets: int32 [2, 256], P(None, 'scan'), may hold values from 0 to 896, as said below
- measured: float32 [256, 128, 128], P('scan'), may hold values from 0.05 to 3
Outputs:
- object_new: float32 [2, 2048, 1024], P(None, ('scan', 'mode'))
- probe_new: float32 [2, 32, 128, 128], P(None, 'mode')
Inputs may be any that keep to these rules, and one draw needn't show every extreme that they name: scan_offsets[0, j] lies in 0 to 128 and scan_offsets[1, j] in 0 to 896; position j belongs to tile j // 32.
All inputs are finite; a program needn't handle non-finite values.
Results may differ from a plain program's by a relative error of at most 0.0027.
Values sent between devices are 32-bit elements; how exact they have to be, the bound alone decides.
No kernel may reach another device: no remote copies, remote signals or barrier semaphores. Data moves between devices by JAX's collectives and lax.ppermute only.
A program may use at most 128 MiB of HBM per device.

v0:
```python
import math
import jax
import jax.numpy as jnp
from jax import lax
from jax.sharding import PartitionSpec as P

M = 128
NS_ITERS = 8
FLOOR_INTENSITY = 0.1
FLOOR_ILLUM = 1.0
EPSILON = 1e-06


def dft_tables(length):
    pixel_index = jnp.arange(length, dtype=jnp.int32)
    product = pixel_index[:, None] * pixel_index[None, :] % length
    phase_angle = product.astype(jnp.float32) * (2.0 * math.pi / length)
    norm_scale = 1.0 / math.sqrt(length)
    return (
        (jnp.cos(phase_angle) * norm_scale).astype(jnp.bfloat16),
        (-jnp.sin(phase_angle) * norm_scale).astype(jnp.bfloat16),
    )


def right_product(left, table):
    return jnp.einsum("nab,bc->nac", left, table, preferred_element_type=jnp.float32)


def left_product(table, right):
    return jnp.einsum("ab,nbc->nac", table, right, preferred_element_type=jnp.float32)


def forward_pass(wave_re, wave_im, cos_t, sin_t):
    mid_re = (right_product(wave_re, cos_t) - right_product(wave_im, sin_t)).astype(jnp.bfloat16)
    mid_im = (right_product(wave_re, sin_t) + right_product(wave_im, cos_t)).astype(jnp.bfloat16)
    far_re = left_product(cos_t, mid_re) - left_product(sin_t, mid_im)
    far_im = left_product(sin_t, mid_re) + left_product(cos_t, mid_im)
    return (far_re, far_im)


def inverse_pass(spec_re, spec_im, cos_t, sin_t):
    half_re = (right_product(spec_re, cos_t) + right_product(spec_im, sin_t)).astype(jnp.bfloat16)
    half_im = (right_product(spec_im, cos_t) - right_product(spec_re, sin_t)).astype(jnp.bfloat16)
    back_re = left_product(cos_t, half_re) + left_product(sin_t, half_im)
    back_im = left_product(cos_t, half_im) - left_product(sin_t, half_re)
    return (back_re, back_im)


def highest_dot(left, right):
    return jnp.dot(left, right, precision=lax.Precision.HIGHEST, preferred_element_type=jnp.float32)


def gram_of(flat_re, flat_im):
    gram_re = highest_dot(flat_re, flat_re.T) + highest_dot(flat_im, flat_im.T)
    gram_im = highest_dot(flat_re, flat_im.T) - highest_dot(flat_im, flat_re.T)
    return (gram_re, gram_im)


def orthogonal_mix(gram_re, gram_im):
    mode_count = gram_re.shape[0]
    mode_power = jnp.diagonal(gram_re) + EPSILON
    inv_root = 1.0 / jnp.sqrt(mode_power)
    scale_mat = inv_root[:, None] * inv_root[None, :]
    norm_re = gram_re * scale_mat
    norm_im = gram_im * scale_mat
    embedded = jnp.concatenate(
        [jnp.concatenate([norm_re, -norm_im], axis=1), jnp.concatenate([norm_im, norm_re], axis=1)],
        axis=0,
    )
    frobenius = jnp.sqrt(jnp.sum(embedded * embedded))
    identity_mat = jnp.eye(2 * mode_count, dtype=jnp.float32)
    iterate_y = embedded / frobenius
    iterate_z = identity_mat
    for sweep_index in range(NS_ITERS):
        correction = 1.5 * identity_mat - 0.5 * highest_dot(iterate_z, iterate_y)
        iterate_y = highest_dot(iterate_y, correction)
        iterate_z = highest_dot(correction, iterate_z)
    root_inv = iterate_z / jnp.sqrt(frobenius)
    weight_re = root_inv[:mode_count, :mode_count]
    weight_im = root_inv[mode_count:, :mode_count]
    ratio_mat = inv_root[:, None] * jnp.sqrt(mode_power)[None, :]
    return (weight_re * ratio_mat, weight_im * ratio_mat)


def onehot_place(starts, out_len, in_len):
    out_index = jnp.arange(out_len, dtype=jnp.int32)[None, :, None]
    in_index = jnp.arange(in_len, dtype=jnp.int32)[None, None, :]
    return (out_index == starts[:, None, None] + in_index).astype(jnp.bfloat16)


def split_parts(values):
    high = values.astype(jnp.bfloat16)
    rest = values - high.astype(jnp.float32)
    middle = rest.astype(jnp.bfloat16)
    low = (rest - middle.astype(jnp.float32)).astype(jnp.bfloat16)
    return jnp.stack([high, middle, low])


def shards(object_field, probe_modes, scan_offsets, measured):
    mode_index = lax.axis_index("mode")
    cos_t, sin_t = dft_tables(M)
    probe_re = probe_modes[0, 0]
    probe_im = probe_modes[1, 0]
    row_starts = scan_offsets[0]
    col_starts = scan_offsets[1]
    local_count = row_starts.shape[0]
    zero_index = jnp.zeros((), jnp.int32)

    def cut_patch(row_start, col_start):
        return lax.dynamic_slice(object_field, (zero_index, row_start, col_start), (2, M, M))

    obj_patches = jax.vmap(cut_patch)(row_starts, col_starts)
    obj_re = obj_patches[:, 0]
    obj_im = obj_patches[:, 1]
    obj_norm = jnp.sum(obj_re * obj_re + obj_im * obj_im, axis=0)
    wave_re = (probe_re * obj_re - probe_im * obj_im).astype(jnp.bfloat16)
    wave_im = (probe_re * obj_im + probe_im * obj_re).astype(jnp.bfloat16)
    far_re, far_im = forward_pass(wave_re, wave_im, cos_t, sin_t)
    mode_intensity = far_re * far_re + far_im * far_im
    own_light = (probe_re * probe_re + probe_im * probe_im)[None]
    summed = lax.psum(jnp.concatenate([mode_intensity, own_light]), "mode")
    intensity = summed[:local_count]
    light_patch = summed[local_count:]
    amp_ratio = jnp.sqrt(measured / jnp.maximum(intensity, FLOOR_INTENSITY))
    factor = amp_ratio - 1.0
    spec_re = (factor * far_re).astype(jnp.bfloat16)
    spec_im = (factor * far_im).astype(jnp.bfloat16)
    back_re, back_im = inverse_pass(spec_re, spec_im, cos_t, sin_t)
    grad_re = jnp.sum(obj_re * back_re + obj_im * back_im, axis=0)
    grad_im = jnp.sum(obj_re * back_im - obj_im * back_re, axis=0)
    patch_re = probe_re * back_re + probe_im * back_im
    patch_im = probe_re * back_im - probe_im * back_re
    grad_re, grad_im, obj_norm = lax.psum((grad_re, grad_im, obj_norm), "scan")
    step_re = probe_re + grad_re / (obj_norm + EPSILON)
    step_im = probe_im + grad_im / (obj_norm + EPSILON)
    rows_share = object_field.shape[1] // lax.axis_size("mode")
    col_place = onehot_place(col_starts, object_field.shape[2], M)
    row_place = onehot_place(row_starts, object_field.shape[1], M)
    patch_parts = split_parts(jnp.stack([patch_re, patch_im]))
    placed_rows = jnp.einsum(
        "jia,pcjab->pcjib", row_place, patch_parts, preferred_element_type=jnp.float32
    ).astype(jnp.bfloat16)
    grad_tile = jnp.einsum(
        "pcjib,jkb->pcik", placed_rows, col_place, preferred_element_type=jnp.float32
    ).sum(axis=0)
    own_place = onehot_place(row_starts - mode_index * rows_share, rows_share, M)
    light_parts = split_parts(light_patch[0])
    light_rows = jnp.einsum(
        "jia,pab->pjib", own_place, light_parts, preferred_element_type=jnp.float32
    ).astype(jnp.bfloat16)
    light_rows = jnp.einsum(
        "pjib,jkb->pik", light_rows, col_place, preferred_element_type=jnp.float32
    ).sum(axis=0)[None]
    grad_rows = lax.psum_scatter(grad_tile, "mode", scatter_dimension=1, tiled=True)
    own_rows = lax.dynamic_slice_in_dim(object_field, mode_index * rows_share, rows_share, 1)
    object_new = own_rows + grad_rows / jnp.maximum(light_rows, FLOOR_ILLUM)
    flat_mine = jnp.stack([step_re.reshape(-1), step_im.reshape(-1)])[:, None, :]
    every_mode = lax.all_gather(flat_mine, "mode", axis=1, tiled=True)
    gathered_re = every_mode[0]
    gathered_im = every_mode[1]
    gram_re, gram_im = gram_of(gathered_re, gathered_im)
    mix_re, mix_im = orthogonal_mix(gram_re, gram_im)
    column_re = lax.dynamic_slice_in_dim(mix_re, mode_index, 1, 1)
    column_im = lax.dynamic_slice_in_dim(mix_im, mode_index, 1, 1)
    mine_re = highest_dot(column_re.T, gathered_re) - highest_dot(column_im.T, gathered_im)
    mine_im = highest_dot(column_re.T, gathered_im) + highest_dot(column_im.T, gathered_re)
    mine = jnp.stack([mine_re, mine_im])
    probe_new = mine.reshape(2, 1, M, M)
    return (object_new, probe_new)


def solution(mesh):
    placed = (
        P(None, "scan", None),
        P(None, "mode", None, None),
        P(None, "scan"),
        P("scan", None, None),
    )
    return jax.shard_map(
        shards,
        mesh=mesh,
        in_specs=placed,
        out_specs=(P(None, ("scan", "mode"), None), P(None, "mode", None, None)),
        check_vma=False,
    )
```

profile of v0, /device:TPU:2, one launch (start us, length us, event | category | flops | bytes accessed | tf_op | source)
XLA Modules:
  0.0 740.6 jit_solution(13497158749242758823)
XLA Ops:
  9.1 118.7 %while.1 = (s32[]{:T(128)}, f32[2,256,1024]{2,1,0:T(8,128)}, s32[32,3]{0,1:T(4,128)S(1)}, f32[32,2,128,128]{2,3,0,1:T(8,128)}, s32[]{:T(128)}) while((s32[]{:T(128)}, f32[2,256,1024]{2,1,0:T(8,128)}, s32[32,3]{0,1:T(4,128)S(1)}, f32[32,2,128,128]{2,3,0,1:T(8,128)}, s32[]{:T(128)}) %tuple.46), condition=%wide.while_cond, body=%wide.while_body.sunk | while | flops 2 | bytes 786557 | solution.py:110
  9.7 2.3 dynamic-slice_bitcast_fusion.2
  17.1 2.3 dynamic-slice_bitcast_fusion.2
  31.9 2.3 dynamic-slice_bitcast_fusion.2
  35.6 2.3 dynamic-slice_bitcast_fusion.2
  39.4 2.3 dynamic-slice_bitcast_fusion.2
  43.1 2.3 dynamic-slice_bitcast_fusion.2
  57.9 2.3 dynamic-slice_bitcast_fusion.2
  65.3 2.3 dynamic-slice_bitcast_fusion.2
  69.0 2.3 dynamic-slice_bitcast_fusion.2
  76.4 2.3 dynamic-slice_bitcast_fusion.2
  83.8 2.3 dynamic-slice_bitcast_fusion.2
  87.5 2.3 dynamic-slice_bitcast_fusion.2
  91.2 2.3 dynamic-slice_bitcast_fusion.2
  95.0 2.3 dynamic-slice_bitcast_fusion.2
  98.7 2.3 dynamic-slice_bitcast_fusion.2
  127.8 2.8 fusion.44
  139.5 2.9 copy.40
  142.5 154.0 %all-reduce.4.cloned.1.call-done = f32[33,128,128]{1,2,0:T(8,128)} async-done(((f32[33,128,128]{1,2,0:T(8,128)}), f32[33,128,128]{1,2,0:T(8,128)}) %all-reduce.4.cloned.1.call-update) | async-done | bytes 2162704 | tf_op jit(solution)/shard_map/psum | solution.py:121
  296.5 4.0 fusion.40
  306.8 2.7 fusion.35
  309.9 3.1 fusion.26
  313.6 5.2 fusion.320
  318.8 14.9 %bitcast_reduce_fusion = f32[2,256,1024]{2,1,0:T(8,128)} fusion(s32[32,128]{1,0:T(8,128)S(1)} %get-tuple-element.62, bf16[3,2,32,256,128]{4,3,2,1,0:T(8,128)(2,1)S(1)} %fusion.320), kind=kOutput, calls=%fused_computation.19 | convolution fusion | flops 12890144768 | bytes 14696448 | tf_op jit(solution)/shard_map/pcjib,jkb->pcik/dot_general | solution.py:143
  334.0 40.0 %all-reduce.6.cloned.1.call-done = (f32[128,128]{0,1:T(8,128)}, f32[128,128]{0,1:T(8,128)}, f32[128,128]{0,1:T(8,128)}) async-done(((f32[128,128]{0,1:T(8,128)}, f32[128,128]{0,1:T(8,128)}, f32[128,128]{0,1:T(8,128)}), (f32[128,128]{0,1:T(8,128)}, f32[128,128]{0,1:T(8,128)}, f32[128,128]{0,1:T(8,128)})) %all-reduce.6.cloned.1.call-update) | async-done | bytes 196624 | tf_op jit(solution)/shard_map/psum | solution.py:133
  376.8 3.2 fusion.61
  380.0 217.7 %reduce-scatter.2.cloned.1.call-done = f32[2,8,1024]{2,1,0:T(8,128)} async-done(((f32[2,256,1024]{2,1,0:T(8,128)}), f32[2,8,1024]{2,1,0:T(8,128)}) %reduce-scatter.2.cloned.1.call-update) | async-done | bytes 65552 | tf_op jit(solution)/shard_map/reduce_scatter | solution.py:154
  599.2 81.5 %all-gather.3.cloned.1.call-done = f32[2,524288]{1,0:T(2,128)} async-done(((f32[2,16384]{1,0:T(2,128)}), f32[2,524288]{1,0:T(2,128)}) %all-gather.3.cloned.1.call-update) | async-done | bytes 4194320 | tf_op jit(solution)/shard_map/all_gather | solution.py:158
  680.8 26.1 %slice_reduce_fusion.1 = (f32[524288]{0:T(1024)}, f32[524288]{0:T(1024)}) fusion(f32[2,524288]{1,0:T(2,128)} %all-gather.3.cloned.1.call-done), kind=kLoop, calls=%fused_computation.29 | loop fusion | bytes 8388608 | tf_op jit(solution)/shard_map/slice | solution.py:159
  710.4 3.0 squeeze.26
  713.4 3.5 fusion.223
  719.6 3.4 fusion.219
  (236 shorter events, 121.9 us)
Async XLA Ops:
  7.2 289.3 %all-reduce.4.cloned.1.call-start = ((), (), s32[]{:S(2)}) async-start(), calls=%async_computation.1 | async-start | bytes 4325376 | tf_op jit(solution)/shard_map/psum | solution.py:121
  139.1 234.8 %all-reduce.6.cloned.1.call-start = ((), (), s32[]{:S(2)}) async-start(), calls=%async_computation.4 | async-start | bytes 393216 | tf_op jit(solution)/shard_map/psum | solution.py:133
  139.5 2.9 copy-start.3
  304.6 2.2 copy-start.2
  313.0 284.7 %reduce-scatter.2.cloned.1.call-start = ((), (), s32[]{:S(2)}) async-start(), calls=%async_computation.2 | async-start | bytes 2162688 | tf_op jit(solution)/shard_map/reduce_scatter | solution.py:154
  333.7 347.0 %all-gather.3.cloned.1.call-start = ((), (), s32[]{:S(2)}) async-start(), calls=%async_computation.3 | async-start | bytes 4325376 | tf_op jit(solution)/shard_map/all_gather | solution.py:158
  713.4 3.6 copy-start
  725.2 4.6 copy-start.1
Sparse Core Ops, SparseCore 0:
  139.2 157.2 all-reduce.3
  313.2 60.7 all-reduce.5
  377.8 219.9 reduce-scatter.1
  600.8 79.9 all-gather.2
where the time goes:
time: 751 us; the launch traced here: 741 us
  waiting for transfers between devices  493 us (66%)
  local copies, waits for them, and re-layouts  155 us (21%)
  matrix products  56.6 us (8%)
  other arithmetic  18.5 us (2%)
  between operations  15.2 us (2%)
    reduce_scatter x1, waiting for transfers between devices, shards(): lax.psum_scatter(grad_tile, 'mode', scatter_dimension=1, tiled=True)  218 us
    psum x1, waiting for transfers between devices, shards(): summed = lax.psum(jnp.concatenate([mode_intensity, own_light]), 'mode')  154 us
    gather x160, local copies, waits for them, and re-layouts  118 us
    all_gather x1, waiting for transfers between devices, shards(): every_mode = lax.all_gather(flat_mine, 'mode', axis=1, tiled=True)  81.5 us
    psum x1, waiting for transfers between devices, shards(): grad_re, grad_im, obj_norm = lax.psum((grad_re, grad_im, obj_norm), 'scan')  40 us
    slice x1, local copies, waits for them, and re-layouts, shards(): gathered_re = every_mode[0]  26.1 us
    dot_general x31, matrix products, highest_dot(): jnp.dot(left, right, precision=lax.Precision.HIGHEST, preferred_element_t...  18.8 us
  transfers between devices with their start and end apart: 4, of which 4 were waited for; matrix products, arithmetic and copies ran while one was open for 4% of the time, Pallas kernels for 0%

commit v1 on v0

--- a/solution.py
+++ b/solution.py
@@ -155,7 +155,10 @@
     own_rows = lax.dynamic_slice_in_dim(object_field, mode_index * rows_share, rows_share, 1)
     object_new = own_rows + grad_rows / jnp.maximum(light_rows, FLOOR_ILLUM)
     flat_mine = jnp.stack([step_re.reshape(-1), step_im.reshape(-1)])[:, None, :]
-    every_mode = lax.all_gather(flat_mine, "mode", axis=1, tiled=True)
+    signs_touch = lambda inputs: jnp.concatenate(
+        lax.all_to_all(jnp.stack(lax.psum(1, "mode") * [inputs]), "mode", 0, 0), 1
+    )
+    every_mode = signs_touch(flat_mine)
     gathered_re = every_mode[0]
     gathered_im = every_mode[1]
     gram_re, gram_im = gram_of(gathered_re, gathered_im)

time: 751 us -> 709 us (0.944)
  waiting for transfers between devices: 493 us -> 448 us
  local copies, waits for them, and re-layouts: 155 us -> 133 us
  matrix products: 56.6 us -> 71.7 us
  starting transfers between devices: 1.15 us -> 10.5 us
    all_gather x1 -> x0, waiting for transfers between devices: 81.5 us -> none  [shards(): every_mode = lax.all_gather(flat_mine, 'mode', axis=1, tiled=True)]
    slice x1, local copies, waits for them, and re-layouts: 26.1 us -> 2.5 us  [shards(): gathered_re = every_mode[0]]
    reduce_scatter x1, waiting for transfers between devices: 218 us -> 236 us  [shards(): lax.psum_scatter(grad_tile, 'mode', scatter_dimension=1, tiled=True)]
    psum x1, waiting for transfers between devices: 40 us -> 57.6 us  [shards(): grad_re, grad_im, obj_norm = lax.psum((grad_re, grad_im, obj_norm), 'scan')]
    all_to_all x0 -> x1, starting transfers between devices: none -> 9.98 us  [shards(): lax.all_to_all(jnp.stack(lax.psum(1, 'mode') * [inputs]), 'mode', 0, 0)]
    dot_general x31, matrix products: 18.8 us -> 28.6 us  [highest_dot(): jnp.dot(left, right, precision=lax.Precision.HIGHEST, preferred_element_t...]
  transfers between devices with their start and end apart: 4 -> 4, of which waited for: 4 -> 3; matrix products, arithmetic and copies ran while one was open for 4% -> 6% of each run, Pallas kernels for 0% -> 0%
where the time goes in v1:
time: 709 us; the launch traced here: 700 us
  waiting for transfers between devices  448 us (63%)
  local copies, waits for them, and re-layouts  133 us (19%)
  matrix products  71.7 us (10%)
  other arithmetic  20.5 us (3%)
  between operations  15.2 us (2%)
  starting transfers between devices  10.5 us (1%)
    reduce_scatter x1, waiting for transfers between devices, shards(): lax.psum_scatter(grad_tile, 'mode', scatter_dimension=1, tiled=True)  236 us
    psum x1, waiting for transfers between devices, shards(): summed = lax.psum(jnp.concatenate([mode_intensity, own_light]), 'mode')  154 us
    gather x160, local copies, waits for them, and re-layouts  119 us
    psum x1, waiting for transfers between devices, shards(): grad_re, grad_im, obj_norm = lax.psum((grad_re, grad_im, obj_norm), 'scan')  57.6 us
    dot_general x31, matrix products, highest_dot(): jnp.dot(left, right, precision=lax.Precision.HIGHEST, preferred_element_t...  28.6 us
    dot_general x1, matrix products, shards(): jnp.einsum('pcjib,jkb->pcik', placed_rows, col_place, preferred_element_t...  17.8 us
  transfers between devices with their start and end apart: 4, of which 3 were waited for; matrix products, arithmetic and copies ran while one was open for 6% of the time, Pallas kernels for 0%

profile of v1, /device:TPU:2, one launch (start us, length us, event | category | flops | bytes accessed | tf_op | source)
XLA Modules:
  0.0 699.6 jit_solution(12897498428507521943)
XLA Ops:
  9.1 119.0 %while.1 = (s32[]{:T(128)}, f32[2,256,1024]{2,1,0:T(8,128)}, s32[32,3]{0,1:T(4,128)S(1)}, f32[32,2,128,128]{2,3,0,1:T(8,128)}, s32[]{:T(128)}) while((s32[]{:T(128)}, f32[2,256,1024]{2,1,0:T(8,128)}, s32[32,3]{0,1:T(4,128)S(1)}, f32[32,2,128,128]{2,3,0,1:T(8,128)}, s32[]{:T(128)}) %tuple.46), condition=%wide.while_cond, body=%wide.while_body.sunk | while | flops 2 | bytes 786557 | solution.py:110
  9.7 2.3 dynamic-slice_bitcast_fusion.2
  13.4 2.3 dynamic-slice_bitcast_fusion.2
  17.2 2.3 dynamic-slice_bitcast_fusion.2
  20.9 2.3 dynamic-slice_bitcast_fusion.2
  24.6 2.3 dynamic-slice_bitcast_fusion.2
  28.3 2.3 dynamic-slice_bitcast_fusion.2
  46.9 2.3 dynamic-slice_bitcast_fusion.2
  50.6 2.3 dynamic-slice_bitcast_fusion.2
  58.1 2.3 dynamic-slice_bitcast_fusion.2
  65.5 2.3 dynamic-slice_bitcast_fusion.2
  69.2 2.3 dynamic-slice_bitcast_fusion.2
  128.1 2.8 fusion.62
  139.6 2.9 copy.40
  142.7 154.2 %all-reduce.4.cloned.1.call-done = f32[33,128,128]{1,2,0:T(8,128)} async-done(((f32[33,128,128]{1,2,0:T(8,128)}), f32[33,128,128]{1,2,0:T(8,128)}) %all-reduce.4.cloned.1.call-update) | async-done | bytes 2162704 | tf_op jit(solution)/shard_map/psum | solution.py:121
  296.9 4.0 fusion.58
  307.2 4.1 fusion.53
  311.3 3.3 fusion.25
  314.6 57.6 %all-reduce.6.cloned.1.call-done = (f32[128,128]{0,1:T(8,128)}, f32[128,128]{0,1:T(8,128)}, f32[128,128]{0,1:T(8,128)}) async-done(((f32[128,128]{0,1:T(8,128)}, f32[128,128]{0,1:T(8,128)}, f32[128,128]{0,1:T(8,128)}), (f32[128,128]{0,1:T(8,128)}, f32[128,128]{0,1:T(8,128)}, f32[128,128]{0,1:T(8,128)})) %all-reduce.6.cloned.1.call-update) | async-done | bytes 196624 | tf_op jit(solution)/shard_map/psum | solution.py:133
  373.4 6.0 stack.42
  379.4 10.0 %all-to-all-start = ((f32[32,2,1,16384]{3,2,1,0:T(1,128)}), f32[32,2,1,16384]{3,2,1,0:T(1,128)}, u32[]{:S(2)}, u32[]{:S(2)}) async-start(f32[32,2,1,16384]{3,2,1,0:T(1,128)} %stack.42), calls=%async_computation.1 | async-start | bytes 8388608 | tf_op jit(solution)/shard_map/all_to_all | solution.py:159
  389.7 2.9 fusion.26
  392.6 6.3 fusion.343
  398.9 17.8 %bitcast_reduce_fusion = f32[2,256,1024]{2,1,0:T(8,128)} fusion(s32[32,128]{1,0:T(8,128)S(1)} %get-tuple-element.62, bf16[3,2,32,256,128]{4,3,2,1,0:T(8,128)(2,1)} %fusion.343), kind=kOutput, calls=%fused_computation.19 | convolution fusion | flops 12890144768 | bytes 14696448 | tf_op jit(solution)/shard_map/pcjib,jkb->pcik/dot_general | solution.py:143
  417.6 3.2 fusion.89
  420.9 236.0 %reduce-scatter.2.cloned.1.call-done = f32[2,8,1024]{2,1,0:T(8,128)} async-done(((f32[2,256,1024]{2,1,0:T(8,128)}), f32[2,8,1024]{2,1,0:T(8,128)}) %reduce-scatter.2.cloned.1.call-update) | async-done | bytes 65552 | tf_op jit(solution)/shard_map/reduce_scatter | solution.py:154
  658.3 2.5 fusion.253
  660.9 2.8 fusion.38
  663.7 4.2 fusion.34
  667.9 3.0 fusion.100
  671.7 5.6 fusion.256
  687.5 2.4 fusion.40
  (236 shorter events, 126.9 us)
Async XLA Ops:
  7.2 289.7 %all-reduce.4.cloned.1.call-start = ((), (), s32[]{:S(2)}) async-start(), calls=%async_computation.2 | async-start | bytes 4325376 | tf_op jit(solution)/shard_map/psum | solution.py:121
  139.4 232.8 %all-reduce.6.cloned.1.call-start = ((), (), s32[]{:S(2)}) async-start(), calls=%async_computation.4 | async-start | bytes 393216 | tf_op jit(solution)/shard_map/psum | solution.py:133
  139.6 2.9 copy-start.4
  305.0 2.2 copy-start.2
  379.4 278.9 %all-to-all-start = ((f32[32,2,1,16384]{3,2,1,0:T(1,128)}), f32[32,2,1,16384]{3,2,1,0:T(1,128)}, u32[]{:S(2)}, u32[]{:S(2)}) async-start(f32[32,2,1,16384]{3,2,1,0:T(1,128)} %stack.42), calls=%async_computation.1 | async-start | bytes 8388608 | tf_op jit(solution)/shard_map/all_to_all | solution.py:159
  389.4 267.4 %reduce-scatter.2.cloned.1.call-start = ((), (), s32[]{:S(2)}) async-start(), calls=%async_computation.3 | async-start | bytes 2162688 | tf_op jit(solution)/shard_map/reduce_scatter | solution.py:154
  389.7 2.9 copy-start.3
  660.8 7.0 %copy-start = (f32[1,32,1,16384]{3,2,0,1:T(1,128)}, f32[1,32,1,16384]{3,2,0,1:T(1,128)S(1)}, u32[]{:S(2)}) copy-start(f32[1,32,1,16384]{3,2,0,1:T(1,128)S(1)} %get-tuple-element.37) | copy-start | bytes 6291460
  678.7 4.2 copy-start.1
Sparse Core Ops, SparseCore 0:
  139.5 157.3 all-reduce.3
  311.4 60.6 all-reduce.5
  416.8 239.9 reduce-scatter.1
